TPU v7x, 256 devices: a whole 4x4x8 slice. The times are simulated.
256 devices in a mesh: dp: 8 (over x, core), seq: 32 (over y, z).
Axes of the slice: x: 4, y: 4, z: 8, core: 2. Of those that a mesh axis runs over, the one named last changes fastest.
Arguments:
- activations: bfloat16 [8, 4096, 2048], P('dp', 'seq'), may hold values from -16 to 16
- w_query: bfloat16 [2048, 2048], P('seq')
- w_key: bfloat16 [2048, 256], P('seq')
- w_value: bfloat16 [2048, 256], P('seq'), may hold values from -0.125 to 0.125
- key_blocks: int32 [32, 32, 7], replicated, may hold values from 0 to 31, as said below
- random_count: int32 [32], replicated, may hold values from 1 to 3, 64 in all
- grad_out: bfloat16 [8, 4096, 2048], P('dp', 'seq'), may hold values from -6 to 6
Outputs:
- attn_out: bfloat16 [8, 4096, 2048], P('dp', 'seq')
- grad_x: bfloat16 [8, 4096, 2048], P('dp', 'seq')
- grad_wq: bfloat16 [2048, 2048], P('seq')
- grad_wk: bfloat16 [2048, 256], P('seq')
- grad_wv: bfloat16 [2048, 256], P('seq')
Inputs may be any that keep to these rules, and one draw needn't show every extreme that they name: `key_blocks`: row b of head h: columns 0 to 2 are b - 1, b and b + 1 modulo 32; column 3 is one block of the head, the same in all its rows; columns 4 to 6 are three blocks that differ from each other and from the row's first four entries. Head h uses the first random_count[h] of its three random key blocks; the counts sum to 64.
All inputs are finite; a program needn't handle non-finite values.
Results may differ from a plain program's by a relative error of at most 0.025.
The roundings to bfloat16 on the way count: a program that leaves them out, or rounds other values in their place, can miss the bound.
Values may be sent and summed in bfloat16 or wider, within the bound.
No kernel may reach another device: no remote copies, remote signals or barrier semaphores. Data moves between devices by JAX's collectives and lax.ppermute only.
A program may use at most 128 MiB of HBM per device.

v0:
```python
import math
import jax
import jax.numpy as jnp
from jax import lax
from jax.sharding import PartitionSpec as P

HD = 64
GROUP = 8
masked_score = -1e30
query_group = 4


def head_pass(queries, key_rows, value_rows, grad_head, blocks, extra_count):
    seq_len, head_width = queries.shape
    block_count, slot_count = blocks.shape
    block_len = seq_len // block_count
    score_scale = head_width ** (-0.5)
    key_tiles = key_rows.reshape(block_count, block_len, head_width)
    value_tiles = value_rows.reshape(block_count, block_len, head_width)
    usable = jnp.repeat(jnp.arange(slot_count) < 4 + extra_count, block_len)
    rounds = block_count // query_group
    query_steps = queries.reshape(rounds, query_group, block_len, head_width)
    grad_steps = grad_head.reshape(rounds, query_group, block_len, head_width)
    block_steps = blocks.reshape(rounds, query_group, slot_count)

    def one_step(running, inputs):
        q_part, g_part, chosen = inputs
        k_part = key_tiles[chosen].reshape(query_group, slot_count * block_len, head_width)
        v_part = value_tiles[chosen].reshape(query_group, slot_count * block_len, head_width)
        scores = (
            jnp.einsum("gqe,gke->gqk", q_part, k_part, preferred_element_type=jnp.float32)
            * score_scale
        )
        scores = jnp.where(usable, scores, masked_score)
        highest = jnp.max(scores, axis=-1, keepdims=True)
        exponent = jnp.exp(scores - highest)
        shares = exponent / jnp.sum(exponent, axis=-1, keepdims=True)
        shares_low = shares.astype(jnp.bfloat16)
        attended = jnp.einsum(
            "gqk,gke->gqe", shares_low, v_part, preferred_element_type=jnp.float32
        ).astype(jnp.bfloat16)
        grad_shares = jnp.einsum("gqe,gke->gqk", g_part, v_part, preferred_element_type=jnp.float32)
        weighted = jnp.sum(grad_shares * shares, axis=-1, keepdims=True)
        grad_scores = (shares * (grad_shares - weighted)).astype(jnp.bfloat16)
        grad_query = (
            jnp.einsum("gqk,gke->gqe", grad_scores, k_part, preferred_element_type=jnp.float32)
            * score_scale
        ).astype(jnp.bfloat16)
        grad_keys = (
            jnp.einsum("gqk,gqe->gke", grad_scores, q_part, preferred_element_type=jnp.float32)
            * score_scale
        )
        grad_values = jnp.einsum(
            "gqk,gqe->gke", shares_low, g_part, preferred_element_type=jnp.float32
        )
        pieces = jnp.concatenate([grad_keys, grad_values], axis=-1).reshape(
            query_group * slot_count, block_len, 2 * head_width
        )
        running = running.at[chosen.reshape(-1)].add(pieces)
        return (running, (attended, grad_query))

    initial = jnp.zeros((block_count, block_len, 2 * head_width), jnp.float32)
    summed, (attended, grad_query) = lax.scan(
        one_step, initial, (query_steps, grad_steps, block_steps)
    )
    return (
        attended.reshape(seq_len, head_width),
        grad_query.reshape(seq_len, head_width),
        summed.reshape(seq_len, 2 * head_width),
    )


def per_device(activations, w_query, w_key, w_value, key_blocks, random_count, grad_out):
    seq_devices = lax.axis_size("seq")
    dp_devices = lax.axis_size("dp")
    position = lax.axis_index("seq")
    dp_index = lax.axis_index("dp")
    tokens = activations[0]
    grad_rows = grad_out[0]
    tok_count = tokens.shape[0]
    heads = w_query.shape[1] // HD
    kv_heads = w_key.shape[1] // HD
    query_cols = heads * HD
    kv_cols = kv_heads * HD
    all_cols = query_cols + 2 * kv_cols
    w_local = jnp.concatenate([w_query, w_key, w_value], axis=1)
    w_full = lax.all_gather(w_local, "seq", axis=0, tiled=True)
    projected = jnp.dot(tokens, w_full, preferred_element_type=jnp.float32).astype(jnp.bfloat16)
    queries = projected[:, :query_cols]
    key_proj = projected[:, query_cols : query_cols + kv_cols]
    value_proj = projected[:, query_cols + kv_cols :]
    query_pieces = queries.reshape(tok_count, heads, HD).transpose(1, 0, 2)
    grad_pieces = grad_rows.reshape(tok_count, heads, HD).transpose(1, 0, 2)
    paired = jnp.concatenate(
        [key_proj.reshape(tok_count, kv_heads, HD), value_proj.reshape(tok_count, kv_heads, HD)],
        axis=2,
    )
    kv_pieces = jnp.repeat(paired.transpose(1, 0, 2), GROUP, axis=0)
    sent = jnp.concatenate([query_pieces, grad_pieces, kv_pieces], axis=2)
    landed = lax.all_to_all(sent, "seq", split_axis=0, concat_axis=1, tiled=True)[0]
    head_q = landed[:, :HD]
    head_grad = landed[:, HD : 2 * HD]
    head_k = landed[:, 2 * HD : 3 * HD]
    head_v = landed[:, 3 * HD :]
    blocks_mine = lax.dynamic_index_in_dim(key_blocks, position, 0, keepdims=False)
    count_mine = lax.dynamic_index_in_dim(random_count, position, 0, keepdims=False)
    attended, grad_query, grad_kv = head_pass(
        head_q, head_k, head_v, head_grad, blocks_mine, count_mine
    )
    back_sent = jnp.concatenate(
        [
            attended.reshape(seq_devices, tok_count, HD),
            grad_query.reshape(seq_devices, tok_count, HD),
            grad_kv.astype(jnp.bfloat16).reshape(seq_devices, tok_count, 2 * HD),
        ],
        axis=2,
    )
    back = lax.all_to_all(back_sent, "seq", split_axis=0, concat_axis=0, tiled=True)
    back_out = back[:, :, :HD]
    back_query = back[:, :, HD : 2 * HD]
    back_kv = back[:, :, 2 * HD :]
    out_rows = back_out.transpose(1, 0, 2).reshape(tok_count, heads * HD)
    grad_q_rows = back_query.transpose(1, 0, 2).reshape(tok_count, heads * HD)
    kv_sum = jnp.sum(
        back_kv.reshape(kv_heads, GROUP, tok_count, 2 * HD), axis=1, dtype=jnp.float32
    ).astype(jnp.bfloat16)
    grad_k_rows = kv_sum[:, :, :HD].transpose(1, 0, 2).reshape(tok_count, kv_heads * HD)
    grad_v_rows = kv_sum[:, :, HD:].transpose(1, 0, 2).reshape(tok_count, kv_heads * HD)
    combined = jnp.concatenate([grad_q_rows, grad_k_rows, grad_v_rows], axis=1)
    contract = (((1,), (1,)), ((), ()))
    grad_x_rows = lax.dot_general(
        combined, w_full, contract, preferred_element_type=jnp.float32
    ).astype(jnp.bfloat16)
    factor = 1.0 / math.sqrt(tok_count * seq_devices * dp_devices)
    over_tokens = (((0,), (0,)), ((), ()))
    term = (
        lax.dot_general(tokens, combined, over_tokens, preferred_element_type=jnp.float32) * factor
    ).astype(jnp.bfloat16)
    half = all_cols // 2
    core = dp_index % 2
    pairs = [(i, i ^ 1) for i in range(dp_devices)]
    keep = lax.dynamic_slice_in_dim(term, core * half, half, axis=1)
    give = lax.dynamic_slice_in_dim(term, (1 - core) * half, half, axis=1)
    got = lax.ppermute(give, "dp", pairs)
    chip_sum = (keep.astype(jnp.float32) + got.astype(jnp.float32)).astype(jnp.bfloat16)
    part = lax.psum_scatter(chip_sum, "seq", scatter_dimension=0, tiled=True)
    step = 2
    while step < dp_devices:
        mates = [(i, i ^ step) for i in range(dp_devices)]
        other = lax.ppermute(part, "dp", mates)
        part = (part.astype(jnp.float32) + other.astype(jnp.float32)).astype(jnp.bfloat16)
        step *= 2
    other_half = lax.ppermute(part, "dp", pairs)
    first = jnp.where(core == 0, part, other_half)
    second = jnp.where(core == 0, other_half, part)
    grad_all = jnp.concatenate([first, second], axis=1)
    grad_wq = grad_all[:, :query_cols]
    grad_wk = grad_all[:, query_cols : query_cols + kv_cols]
    grad_wv = grad_all[:, query_cols + kv_cols :]
    return (out_rows[None], grad_x_rows[None], grad_wq, grad_wk, grad_wv)


def solution(mesh):
    placed = (
        P("dp", "seq", None),
        P("seq", None),
        P("seq", None),
        P("seq", None),
        P(),
        P(),
        P("dp", "seq", None),
    )
    return jax.shard_map(
        per_device,
        mesh=mesh,
        in_specs=placed,
        out_specs=(
            P("dp", "seq", None),
            P("dp", "seq", None),
            P("seq", None),
            P("seq", None),
            P("seq", None),
        ),
        check_vma=False,
    )
```

profile of v0, /device:TPU:7, one launch (start us, length us, event | category | flops | bytes accessed | tf_op | source)
XLA Modules:
  0.0 728.5 jit_solution(3099953773682184216)
XLA Ops:
  7.2 1.8 pad_maximum_fusion.5
  10.4 112.5 %all-gather.2.cloned.1.call-done = bf16[2048,2560]{1,0:T(8,128)(2,1)} async-done(((bf16[64,2560]{1,0:T(8,128)(2,1)}), bf16[2048,2560]{1,0:T(8,128)(2,1)}) %all-gather.2.cloned.1.call-update) | async-done | bytes 10485776 | tf_op jit(solution)/shard_map/all_gather | solution.py:87
  122.8 6.9 fusion.43
  131.6 5.4 all-to-all-start
  139.2 46.5 %all-to-all-done = bf16[32,128,256]{1,2,0:T(8,128)(2,1)S(1)} async-done(((bf16[32,128,256]{1,2,0:T(8,128)(2,1)}), bf16[32,128,256]{1,2,0:T(8,128)(2,1)S(1)}, u32[]{:S(2)}, u32[]{:S(2)}) %all-to-all-start) | async-done | bytes 2097184 | tf_op jit(solution)/shard_map/all_to_all | solution.py:100
  185.7 2.9 copy.68
  188.6 4.2 fusion.53
  192.8 2.3 copy.72
  195.1 2.3 copy.71
  199.0 167.2 %while.15 = (s32[]{:T(128)}, f32[32,128,128]{2,1,0:T(8,128)}, bf16[8,4,128,64]{2,3,1,0:T(8,128)(2,1)}, bf16[8,4,128,64]{2,3,1,0:T(8,128)(2,1)}, s32[8,4,7]{2,1,0...) while((s32[]{:T(128)}, f32[32,128,128]{2,1,0:T(8,128)}, ...), condition=%wide.region_5.6_spmd.clone, body=%wide.region_0.5_spmd.clone.sunk | while | flops 360449568 | bytes 45045204 | solution.py:63
  199.3 1.7 gather_fusion.1
  201.7 1.6 fusion.93
  203.4 2.4 fusion.95
  211.4 1.7 copy.89
  213.1 6.9 scatter_fusion
  220.2 1.7 gather_fusion.1
  224.3 2.4 fusion.95
  232.3 1.7 copy.89
  234.0 6.9 scatter_fusion
  241.1 1.7 gather_fusion.1
  243.6 1.6 fusion.93
  245.2 2.4 fusion.95
  253.2 1.7 copy.89
  254.9 6.8 scatter_fusion
  262.0 1.7 gather_fusion.1
  264.4 1.6 fusion.93
  266.1 2.4 fusion.95
  274.1 1.7 copy.89
  275.8 6.8 scatter_fusion
  282.9 1.7 gather_fusion.1
  285.3 1.6 fusion.93
  287.0 2.4 fusion.95
  295.0 1.7 copy.89
  296.7 6.9 scatter_fusion
  303.8 1.7 gather_fusion.1
  306.3 1.6 fusion.93
  307.9 2.4 fusion.95
  315.9 1.7 copy.89
  317.6 6.8 scatter_fusion
  324.7 1.7 gather_fusion.1
  327.1 1.6 fusion.93
  328.8 2.4 fusion.95
  336.8 1.7 copy.89
  338.5 6.8 scatter_fusion
  345.6 1.7 gather_fusion.1
  348.0 1.6 fusion.93
  349.7 2.4 fusion.95
  357.7 1.7 copy.89
  359.4 6.8 scatter_fusion
  366.2 1.9 copy.73
  369.7 7.2 all-to-all-start.1
  377.1 49.0 %all-to-all-done.1 = bf16[32,128,256]{1,2,0:T(8,128)(2,1)S(1)} async-done(((bf16[32,128,256]{1,2,0:T(8,128)(2,1)}), bf16[32,128,256]{1,2,0:T(8,128)(2,1)S(1)}, u32[]{:S(2)}, u32[]{:S(2)}) %all-to-all-start.1) | async-done | bytes 2097184 | tf_op jit(solution)/shard_map/all_to_all | solution.py:118
  427.2 5.1 multiply_convert_fusion.1
  432.3 3.2 dynamic-slice_bitcast_fusion
  435.5 2.3 copy-done.1
  437.8 1.9 collective-permute-start
  439.7 8.6 %collective-permute-done = bf16[2048,1280]{0,1:T(8,128)(2,1)} collective-permute-done((bf16[2048,1280]{0,1:T(8,128)(2,1)}, bf16[2048,1280]{0,1:T(8,128)(2,1)}, u32[]{:S(2)}, u32[]{:S(2)}) %collective-permute-start) | collective-permute-done | bytes 5242912 | tf_op jit(solution)/shard_map/ppermute | solution.py:144
  448.3 9.4 %fusion.42 = bf16[2048,1280]{0,1:T(8,128)(2,1)} fusion(bf16[2048,1280]{0,1:T(8,128)(2,1)} %collective-permute-done, bf16[2560,2048]{1,0:T(8,128)(2,1)} %copy-done.1, s32[]{:T(128)S(6)} %select_n.59), kind=kLoop, calls=%fused_computation.54 | loop fusion | flops 10485760 | bytes 15728644 | tf_op jit(solution)/shard_map/convert_element_type | solution.py:145
  457.7 7.9 %copy.86 = bf16[2048,1280]{1,0:T(8,128)(2,1)} copy(bf16[2048,1280]{0,1:T(8,128)(2,1)} %fusion.42) | data formatting | bytes 10485760
  465.7 218.4 %reduce-scatter.4.cloned.1.call-done = bf16[64,1280]{1,0:T(8,128)(2,1)} async-done(((bf16[2048,1280]{1,0:T(8,128)(2,1)}), bf16[64,1280]{1,0:T(8,128)(2,1)}) %reduce-scatter.4.cloned.1.call-update) | async-done | bytes 163856
  685.5 5.7 collective-permute-done.1
  692.1 8.1 %collective-permute-done.2 = bf16[64,1280]{0,1:T(8,128)(2,1)S(1)} collective-permute-done((bf16[64,1280]{0,1:T(8,128)(2,1)S(1)}, bf16[64,1280]{0,1:T(8,128)(2,1)S(1)}, u32[]{:S(2)}, u32[]{:S(2)}) %collective-permute-start.2) | collective-permute-done | bytes 163872 | tf_op jit(solution)/shard_map/ppermute | solution.py:150
  700.4 9.5 %collective-permute-start.3 = (bf16[64,1280]{0,1:T(8,128)(2,1)S(1)}, bf16[64,1280]{0,1:T(8,128)(2,1)S(1)}, u32[]{:S(2)}, u32[]{:S(2)}) collective-permute-start(bf16[64,1280]{0,1:T(8,128)(2,1)S(1)} %add_convert_fusion), channel_id=1, source_target_pairs={{0,32},{32,0},{64,96},{96,64},{128,160},{160,128},{192,224},{224,1... | collective-permute-start | bytes 491528 | tf_op jit(solution)/shard_map/ppermute | solution.py:153
  709.9 8.3 %fusion.44 = bf16[1,128,2048]{2,1,0:T(8,128)(2,1)} fusion(bf16[2048,2560]{1,0:T(8,128)(2,1)} %all-gather.2.cloned.1.call-done, bf16[128,256]{0,1:T(8,128)(2,1)S(1)} %bitcast.151, bf16[128,256]{0,1:T(8,128)(2,1)S(1)} %bitcast.149, bf16[128,2048]{0,1:T(8,128)(2,1)S(1)} %bitcast.141), kind=kOutput, calls=%fused_computation.59 | convolution fusion | flops 1344405504 | bytes 11665408 | tf_op jit(solution)/shard_map/dot_general | solution.py:131
  (230 shorter events, 69.2 us)
Async XLA Ops:
  7.2 115.7 %copy-start = (bf16[1,128,2048]{2,1,0:T(8,128)(2,1)S(1)}, bf16[1,128,2048]{2,1,0:T(8,128)(2,1)}, u32[]{:S(2)}) copy-start(bf16[1,128,2048]{2,1,0:T(8,128)(2,1)} %param.9) | copy-start | bytes 1572868
  7.2 115.7 %all-gather.2.cloned.1.call-start = ((), (), s32[]{:S(2)}) async-start(), calls=%async_computation.3 | async-start | bytes 10813440 | tf_op jit(solution)/shard_map/all_gather | solution.py:87
  131.6 5.5 copy-start.10
  131.6 54.1 %all-to-all-start = ((bf16[32,128,256]{1,2,0:T(8,128)(2,1)}), bf16[32,128,256]{1,2,0:T(8,128)(2,1)S(1)}, u32[]{:S(2)}, u32[]{:S(2)}) async-start(bf16[32,128,256]{1,2,0:T(8,128)(2,1)} %pad_maximum_fusion.1), calls=%async_computation | async-start | bytes 4194304 | tf_op jit(solution)/shard_map/all_to_all | solution.py:100
  199.0 1.9 copy-start.2
  199.0 2.7 copy-start.4
  205.7 1.3 copy-start.6
  213.1 6.9 copy-start.3
  213.1 6.9 copy-start.5
  219.9 2.0 copy-start.2
  219.9 2.7 copy-start.4
  226.7 1.3 copy-start.6
  234.0 6.9 copy-start.3
  234.0 6.9 copy-start.5
  240.9 2.0 copy-start.2
  240.9 2.7 copy-start.4
  247.6 1.3 copy-start.6
  254.9 6.8 copy-start.3
  254.9 6.8 copy-start.5
  261.7 2.0 copy-start.2
  261.7 2.7 copy-start.4
  268.5 1.3 copy-start.6
  275.8 6.8 copy-start.3
  275.8 6.8 copy-start.5
  282.6 2.0 copy-start.2
  282.6 2.7 copy-start.4
  289.4 1.3 copy-start.6
  296.7 6.9 copy-start.3
  296.7 6.9 copy-start.5
  303.6 2.0 copy-start.2
  303.6 2.7 copy-start.4
  310.3 1.3 copy-start.6
  317.6 6.8 copy-start.3
  317.6 6.8 copy-start.5
  324.4 2.0 copy-start.2
  324.4 2.7 copy-start.4
  331.2 1.3 copy-start.6
  338.5 6.8 copy-start.3
  338.5 6.8 copy-start.5
  345.3 2.0 copy-start.2
  345.3 2.7 copy-start.4
  352.1 1.3 copy-start.6
  359.4 6.8 copy-start.3
  359.4 6.8 copy-start.5
  366.2 1.9 copy-start.8
  366.2 2.0 copy-start.9
  369.7 56.4 %all-to-all-start.1 = ((bf16[32,128,256]{1,2,0:T(8,128)(2,1)}), bf16[32,128,256]{1,2,0:T(8,128)(2,1)S(1)}, u32[]{:S(2)}, u32[]{:S(2)}) async-start(bf16[32,128,256]{1,2,0:T(8,128)(2,1)} %pad_maximum_fusion.2), calls=%async_computation.1 | async-start | bytes 4194304 | tf_op jit(solution)/shard_map/all_to_all | solution.py:118
  376.9 307.2 %reduce-scatter.4.cloned.1.call-start = ((), (), s32[]{:S(2)}) async-start(), calls=%async_computation.4 | async-start | bytes 5406720
  432.3 5.5 copy-start.1
  437.8 10.6 %collective-permute-start = (bf16[2048,1280]{0,1:T(8,128)(2,1)}, bf16[2048,1280]{0,1:T(8,128)(2,1)}, u32[]{:S(2)}, u32[]{:S(2)}) collective-permute-start(bf16[2048,1280]{0,1:T(8,128)(2,1)} %dynamic-slice_bitcast_fusion), channel_id=1, source_target_pairs={{0,32},{32,0},{64,96},{96,64},{128,160},{160,128},{192,224},{224,1... | collective-permute-start | bytes 15728648 | tf_op jit(solution)/shard_map/ppermute | solution.py:144
  685.2 6.0 collective-permute-start.1
  691.3 9.0 %collective-permute-start.2 = (bf16[64,1280]{0,1:T(8,128)(2,1)S(1)}, bf16[64,1280]{0,1:T(8,128)(2,1)S(1)}, u32[]{:S(2)}, u32[]{:S(2)}) collective-permute-start(bf16[64,1280]{0,1:T(8,128)(2,1)S(1)} %add_convert_fusion.1), channel_id=1, source_target_pairs={{0,128},{32,160},{64,192},{96,224},{128,0},{160,32},{192,64},{224,... | collective-permute-start | bytes 491528 | tf_op jit(solution)/shard_map/ppermute | solution.py:150
  700.4 17.8 %copy-start.7 = (bf16[32,128,64]{1,2,0:T(8,128)(2,1)S(1)}, bf16[32,128,64]{1,2,0:T(8,128)(2,1)}, u32[]{:S(2)}) copy-start(bf16[32,128,64]{1,2,0:T(8,128)(2,1)} %get-tuple-element.162) | copy-start | bytes 1572868
  700.4 18.8 %collective-permute-start.3 = (bf16[64,1280]{0,1:T(8,128)(2,1)S(1)}, bf16[64,1280]{0,1:T(8,128)(2,1)S(1)}, u32[]{:S(2)}, u32[]{:S(2)}) collective-permute-start(bf16[64,1280]{0,1:T(8,128)(2,1)S(1)} %add_convert_fusion), channel_id=1, source_target_pairs={{0,32},{32,0},{64,96},{96,64},{128,160},{160,128},{192,224},{224,1... | collective-permute-start | bytes 491528 | tf_op jit(solution)/shard_map/ppermute | solution.py:153
Sparse Core Ops, SparseCore 0:
  11.2 111.6 all-gather.1
  465.8 218.2 reduce-scatter.3
where the time goes:
time: 731 us; the launch traced here: 729 us
  waiting for transfers between devices  449 us (61%)
  matrix products  93.4 us (13%)
  other arithmetic  73.4 us (10%)
  local copies, waits for them, and re-layouts  72 us (10%)
  starting transfers between devices  25.4 us (3%)
  between operations  14.9 us (2%)
    unnamed x3, waiting for transfers between devices  218 us
    all_gather x1, waiting for transfers between devices, per_device(): w_full = lax.all_gather(w_local, 'seq', axis=0, tiled=True)  112 us
    scatter-add x8, other arithmetic, one_step(): running = running.at[chosen.reshape(-1)].add(pieces)  54.7 us
    all_to_all x1, waiting for transfers between devices, per_device(): lax.all_to_all(back_sent, 'seq', split_axis=0, concat_axis=0, tiled=True)  49 us
    all_to_all x1, waiting for transfers between devices, per_device(): lax.all_to_all(sent, 'seq', split_axis=0, concat_axis=1, tiled=True)[0]  46.5 us
    unnamed x21, local copies, waits for them, and re-layouts  20.6 us
    dot_general x8, matrix products, one_step(): jnp.einsum('gqk,gke->gqe', shares_low, v_part, preferred_element_type=jnp...  19.1 us
  transfers between devices with their start and end apart: 8, of which 7 were waited for; matrix products, arithmetic and copies ran while one was open for 2% of the time, Pallas kernels for 0%

commit v1 on v0

--- a/solution.py
+++ b/solution.py
@@ -71,6 +71,14 @@
 
 
 def per_device(activations, w_query, w_key, w_value, key_blocks, random_count, grad_out):
+
+    def map_reach(t0, mesh_ax):
+        latest = lax.psum(1, axis_name=mesh_ax)
+        local_part = jnp.stack(latest * [t0], axis=0)
+        item_now = lax.all_to_all(local_part, axis_name=mesh_ax, split_axis=0, concat_axis=0)
+        now = jnp.concatenate(item_now, axis=0)
+        return now
+
     seq_devices = lax.axis_size("seq")
     dp_devices = lax.axis_size("dp")
     position = lax.axis_index("seq")
@@ -84,7 +92,7 @@
     kv_cols = kv_heads * HD
     all_cols = query_cols + 2 * kv_cols
     w_local = jnp.concatenate([w_query, w_key, w_value], axis=1)
-    w_full = lax.all_gather(w_local, "seq", axis=0, tiled=True)
+    w_full = map_reach(w_local, "seq")
     projected = jnp.dot(tokens, w_full, preferred_element_type=jnp.float32).astype(jnp.bfloat16)
     queries = projected[:, :query_cols]
     key_proj = projected[:, query_cols : query_cols + kv_cols]

time: 731 us -> 879 us (1.20)
  waiting for transfers between devices: 449 us -> 573 us
  starting transfers between devices: 25.4 us -> 45.8 us
    all_to_all x0 -> x1, waiting for transfers between devices: none -> 238 us  [map_reach(): lax.all_to_all(local_part, axis_name=mesh_ax, split_axis=0, concat_axis=0)]
    all_gather x1 -> x0, waiting for transfers between devices: 112 us -> none  [per_device(): w_full = lax.all_gather(w_local, 'seq', axis=0, tiled=True)]
    all_to_all x0 -> x1, starting transfers between devices: none -> 11.4 us  [map_reach(): lax.all_to_all(local_part, axis_name=mesh_ax, split_axis=0, concat_axis=0)]
    unnamed x21 -> x23, local copies, waits for them, and re-layouts: 20.6 us -> 19.6 us
    unnamed x3 -> x2, waiting for transfers between devices: 218 us -> 218 us
  transfers between devices with their start and end apart: 8 -> 8, of which waited for: 7 -> 7; matrix products, arithmetic and copies ran while one was open for 2% -> 1% of each run, Pallas kernels for 0% -> 0%
where the time goes in v1:
time: 879 us; the launch traced here: 876 us
  waiting for transfers between devices  573 us (65%)
  matrix products  93.3 us (11%)
  local copies, waits for them, and re-layouts  75.9 us (9%)
  other arithmetic  72.7 us (8%)
  starting transfers between devices  45.8 us (5%)
  between operations  14.9 us (2%)
    all_to_all x1, waiting for transfers between devices, map_reach(): lax.all_to_all(local_part, axis_name=mesh_ax, split_axis=0, concat_axis=0)  238 us
    unnamed x2, waiting for transfers between devices  218 us
    scatter-add x8, other arithmetic, one_step(): running = running.at[chosen.reshape(-1)].add(pieces)  54.7 us
    all_to_all x1, waiting for transfers between devices, per_device(): lax.all_to_all(back_sent, 'seq', split_axis=0, concat_axis=0, tiled=True)  48.6 us
    all_to_all x1, waiting for transfers between devices, per_device(): lax.all_to_all(sent, 'seq', split_axis=0, concat_axis=1, tiled=True)[0]  46.5 us
    unnamed x23, local copies, waits for them, and re-layouts  19.6 us
    dot_general x8, matrix products, one_step(): jnp.einsum('gqk,gke->gqe', shares_low, v_part, preferred_element_type=jnp...  19.1 us
  transfers between devices with their start and end apart: 8, of which 7 were waited for; matrix products, arithmetic and copies ran while one was open for 1% of the time, Pallas kernels for 0%

profile of v1, /device:TPU:7, one launch (start us, length us, event | category | flops | bytes accessed | tf_op | source)
XLA Modules:
  0.0 876.1 jit_solution(1736680714293335547)
XLA Ops:
  8.3 5.0 stack.2
  13.3 11.4 %all-to-all-start = ((bf16[32,64,2560]{2,1,0:T(8,128)(2,1)}), bf16[32,64,2560]{2,1,0:T(8,128)(2,1)}, u32[]{:S(2)}, u32[]{:S(2)}) async-start(bf16[32,64,2560]{2,1,0:T(8,128)(2,1)} %stack.2), calls=%async_computation | async-start | bytes 20971520 | tf_op jit(solution)/shard_map/all_to_all | solution.py:78
  25.0 237.8 %all-to-all-done = bf16[32,64,2560]{2,1,0:T(8,128)(2,1)} async-done(((bf16[32,64,2560]{2,1,0:T(8,128)(2,1)}), bf16[32,64,2560]{2,1,0:T(8,128)(2,1)}, u32[]{:S(2)}, u32[]{:S(2)}) %all-to-all-start) | async-done | bytes 10485792 | tf_op jit(solution)/shard_map/all_to_all | solution.py:78
  262.8 6.9 fusion.43
  271.6 13.3 %all-to-all-start.1 = ((bf16[32,128,256]{1,2,0:T(8,128)(2,1)}), bf16[32,128,256]{1,2,0:T(8,128)(2,1)S(1)}, u32[]{:S(2)}, u32[]{:S(2)}) async-start(bf16[32,128,256]{1,2,0:T(8,128)(2,1)} %pad_maximum_fusion.1), calls=%async_computation.1 | async-start | bytes 4194304 | tf_op jit(solution)/shard_map/all_to_all | solution.py:108
  287.0 46.5 %all-to-all-done.1 = bf16[32,128,256]{1,2,0:T(8,128)(2,1)S(1)} async-done(((bf16[32,128,256]{1,2,0:T(8,128)(2,1)}), bf16[32,128,256]{1,2,0:T(8,128)(2,1)S(1)}, u32[]{:S(2)}, u32[]{:S(2)}) %all-to-all-start.1) | async-done | bytes 2097184 | tf_op jit(solution)/shard_map/all_to_all | solution.py:108
  333.5 2.9 copy.68
  336.4 4.2 fusion.53
  340.6 2.3 copy.72
  342.9 2.3 copy.71
  346.8 167.1 %while.15 = (s32[]{:T(128)}, f32[32,128,128]{2,1,0:T(8,128)}, bf16[8,4,128,64]{2,3,1,0:T(8,128)(2,1)}, bf16[8,4,128,64]{2,3,1,0:T(8,128)(2,1)}, s32[8,4,7]{2,1,0...) while((s32[]{:T(128)}, f32[32,128,128]{2,1,0:T(8,128)}, ...), condition=%wide.region_5.6_spmd.clone, body=%wide.region_0.5_spmd.clone.sunk | while | flops 360449568 | bytes 45045204 | solution.py:63
  347.1 1.7 gather_fusion.1
  349.5 1.6 fusion.93
  351.2 2.4 fusion.95
  359.2 1.7 copy.89
  360.9 6.9 scatter_fusion
  368.0 1.7 gather_fusion.1
  370.4 1.6 fusion.93
  372.1 2.4 fusion.95
  380.1 1.7 copy.89
  381.8 6.9 scatter_fusion
  388.9 1.7 gather_fusion.1
  391.3 1.6 fusion.93
  393.0 2.4 fusion.95
  401.0 1.7 copy.89
  402.7 6.8 scatter_fusion
  409.8 1.7 gather_fusion.1
  412.2 1.6 fusion.93
  413.9 2.4 fusion.95
  421.8 1.7 copy.89
  423.6 6.8 scatter_fusion
  430.7 1.7 gather_fusion.1
  433.1 1.6 fusion.93
  434.7 2.4 fusion.95
  442.7 1.7 copy.89
  444.4 6.9 scatter_fusion
  451.6 1.7 gather_fusion.1
  454.0 1.6 fusion.93
  455.7 2.4 fusion.95
  463.6 1.7 copy.89
  465.4 6.8 scatter_fusion
  472.4 1.7 gather_fusion.1
  476.5 2.4 fusion.95
  484.5 1.7 copy.89
  486.2 6.8 scatter_fusion
  493.3 1.7 gather_fusion.1
  497.4 2.4 fusion.95
  505.4 1.7 copy.89
  507.1 6.8 scatter_fusion
  513.9 1.9 copy.73
  517.4 7.2 all-to-all-start.2
  524.6 48.6 %all-to-all-done.2 = bf16[32,128,256]{1,2,0:T(8,128)(2,1)S(1)} async-done(((bf16[32,128,256]{1,2,0:T(8,128)(2,1)}), bf16[32,128,256]{1,2,0:T(8,128)(2,1)S(1)}, u32[]{:S(2)}, u32[]{:S(2)}) %all-to-all-start.2) | async-done | bytes 2097184 | tf_op jit(solution)/shard_map/all_to_all | solution.py:126
  574.2 5.1 multiply_convert_fusion.1
  579.3 3.2 dynamic-slice_bitcast_fusion
  582.6 2.3 copy-done.1
  584.8 2.5 collective-permute-start
  587.3 8.6 collective-permute-done
  595.9 9.4 %fusion.42 = bf16[2048,1280]{0,1:T(8,128)(2,1)} fusion(bf16[2048,1280]{0,1:T(8,128)(2,1)} %collective-permute-done, bf16[2560,2048]{1,0:T(8,128)(2,1)} %copy-done.1, s32[]{:T(128)S(6)} %select_n.59), kind=kLoop, calls=%fused_computation.54 | loop fusion | flops 10485760 | bytes 15728644 | tf_op jit(solution)/shard_map/convert_element_type | solution.py:153
  605.4 7.9 copy.86
  613.3 218.4 %reduce-scatter.4.cloned.1.call-done = bf16[64,1280]{1,0:T(8,128)(2,1)} async-done(((bf16[2048,1280]{1,0:T(8,128)(2,1)}), bf16[64,1280]{1,0:T(8,128)(2,1)}) %reduce-scatter.4.cloned.1.call-update) | async-done | bytes 163856
  833.4 5.3 collective-permute-done.1
  840.1 7.7 collective-permute-done.2
  848.0 9.5 %collective-permute-start.3 = (bf16[64,1280]{0,1:T(8,128)(2,1)S(1)}, bf16[64,1280]{0,1:T(8,128)(2,1)S(1)}, u32[]{:S(2)}, u32[]{:S(2)}) collective-permute-start(bf16[64,1280]{0,1:T(8,128)(2,1)S(1)} %add_convert_fusion), channel_id=1, source_target_pairs={{0,32},{32,0},{64,96},{96,64},{128,160},{160,128},{192,224},{224,1... | collective-permute-start | bytes 491528 | tf_op jit(solution)/shard_map/ppermute | solution.py:161
  857.5 8.3 fusion.44
  (232 shorter events, 71.4 us)
Async XLA Ops:
  7.2 255.6 %copy-start = (bf16[1,128,2048]{2,1,0:T(8,128)(2,1)S(1)}, bf16[1,128,2048]{2,1,0:T(8,128)(2,1)}, u32[]{:S(2)}) copy-start(bf16[1,128,2048]{2,1,0:T(8,128)(2,1)} %param.9) | copy-start | bytes 1572868
  13.3 11.5 %copy-start.8 = (bf16[1,128,2048]{2,1,0:T(8,128)(2,1)S(1)}, bf16[1,128,2048]{2,1,0:T(8,128)(2,1)}, u32[]{:S(2)}) copy-start(bf16[1,128,2048]{2,1,0:T(8,128)(2,1)} %param.15) | copy-start | bytes 1572868
  13.3 249.5 %all-to-all-start = ((bf16[32,64,2560]{2,1,0:T(8,128)(2,1)}), bf16[32,64,2560]{2,1,0:T(8,128)(2,1)}, u32[]{:S(2)}, u32[]{:S(2)}) async-start(bf16[32,64,2560]{2,1,0:T(8,128)(2,1)} %stack.2), calls=%async_computation | async-start | bytes 20971520 | tf_op jit(solution)/shard_map/all_to_all | solution.py:78
  271.5 13.3 %copy-start.11 = (s32[32]{0:T(128)S(1)}, s32[32]{0:T(128)}, u32[]{:S(2)}) copy-start(s32[32]{0:T(128)} %param.14) | copy-start | bytes 388
  271.6 61.9 %all-to-all-start.1 = ((bf16[32,128,256]{1,2,0:T(8,128)(2,1)}), bf16[32,128,256]{1,2,0:T(8,128)(2,1)S(1)}, u32[]{:S(2)}, u32[]{:S(2)}) async-start(bf16[32,128,256]{1,2,0:T(8,128)(2,1)} %pad_maximum_fusion.1), calls=%async_computation.1 | async-start | bytes 4194304 | tf_op jit(solution)/shard_map/all_to_all | solution.py:108
  346.8 1.9 copy-start.2
  346.8 2.7 copy-start.4
  353.6 1.3 copy-start.6
  360.9 6.9 copy-start.3
  360.9 6.9 copy-start.5
  367.7 2.0 copy-start.2
  367.7 2.7 copy-start.4
  374.5 1.3 copy-start.6
  381.8 6.9 copy-start.3
  381.8 6.9 copy-start.5
  388.7 2.0 copy-start.2
  388.7 2.7 copy-start.4
  395.4 1.3 copy-start.6
  402.7 6.8 copy-start.3
  402.7 6.8 copy-start.5
  409.5 2.0 copy-start.2
  409.5 2.7 copy-start.4
  416.2 1.3 copy-start.6
  423.5 6.8 copy-start.3
  423.6 6.8 copy-start.5
  430.4 2.0 copy-start.2
  430.4 2.7 copy-start.4
  437.1 1.3 copy-start.6
  444.4 6.9 copy-start.3
  444.4 6.9 copy-start.5
  451.3 2.0 copy-start.2
  451.3 2.7 copy-start.4
  458.0 1.3 copy-start.6
  465.4 6.8 copy-start.3
  465.4 6.8 copy-start.5
  472.2 2.0 copy-start.2
  472.2 2.7 copy-start.4
  478.9 1.3 copy-start.6
  486.2 6.8 copy-start.3
  486.2 6.8 copy-start.5
  493.1 2.0 copy-start.2
  493.1 2.7 copy-start.4
  499.8 1.3 copy-start.6
  507.1 6.8 copy-start.3
  507.1 6.8 copy-start.5
  513.9 1.9 copy-start.9
  513.9 2.0 copy-start.10
  517.4 55.8 %all-to-all-start.2 = ((bf16[32,128,256]{1,2,0:T(8,128)(2,1)}), bf16[32,128,256]{1,2,0:T(8,128)(2,1)S(1)}, u32[]{:S(2)}, u32[]{:S(2)}) async-start(bf16[32,128,256]{1,2,0:T(8,128)(2,1)} %pad_maximum_fusion.2), calls=%async_computation.2 | async-start | bytes 4194304 | tf_op jit(solution)/shard_map/all_to_all | solution.py:126
  524.6 307.1 %reduce-scatter.4.cloned.1.call-start = ((), (), s32[]{:S(2)}) async-start(), calls=%async_computation.4 | async-start | bytes 5406720
  579.3 5.5 copy-start.1
  584.8 11.1 %collective-permute-start = (bf16[2048,1280]{0,1:T(8,128)(2,1)}, bf16[2048,1280]{0,1:T(8,128)(2,1)}, u32[]{:S(2)}, u32[]{:S(2)}) collective-permute-start(bf16[2048,1280]{0,1:T(8,128)(2,1)} %dynamic-slice_bitcast_fusion), channel_id=1, source_target_pairs={{0,32},{32,0},{64,96},{96,64},{128,160},{160,128},{192,224},{224,1... | collective-permute-start | bytes 15728648 | tf_op jit(solution)/shard_map/ppermute | solution.py:152
  832.8 6.0 collective-permute-start.1
  838.9 9.0 %collective-permute-start.2 = (bf16[64,1280]{0,1:T(8,128)(2,1)S(1)}, bf16[64,1280]{0,1:T(8,128)(2,1)S(1)}, u32[]{:S(2)}, u32[]{:S(2)}) collective-permute-start(bf16[64,1280]{0,1:T(8,128)(2,1)S(1)} %add_convert_fusion.1), channel_id=1, source_target_pairs={{0,128},{32,160},{64,192},{96,224},{128,0},{160,32},{192,64},{224,... | collective-permute-start | bytes 491528 | tf_op jit(solution)/shard_map/ppermute | solution.py:158
  847.9 17.8 %copy-start.7 = (bf16[32,128,64]{1,2,0:T(8,128)(2,1)S(1)}, bf16[32,128,64]{1,2,0:T(8,128)(2,1)}, u32[]{:S(2)}) copy-start(bf16[32,128,64]{1,2,0:T(8,128)(2,1)} %get-tuple-element.162) | copy-start | bytes 1572868
  848.0 18.8 %collective-permute-start.3 = (bf16[64,1280]{0,1:T(8,128)(2,1)S(1)}, bf16[64,1280]{0,1:T(8,128)(2,1)S(1)}, u32[]{:S(2)}, u32[]{:S(2)}) collective-permute-start(bf16[64,1280]{0,1:T(8,128)(2,1)S(1)} %add_convert_fusion), channel_id=1, source_target_pairs={{0,32},{32,0},{64,96},{96,64},{128,160},{160,128},{192,224},{224,1... | collective-permute-start | bytes 491528 | tf_op jit(solution)/shard_map/ppermute | solution.py:161
Sparse Core Ops, SparseCore 0:
  613.4 218.1 reduce-scatter.3
